TPU v7x, 512 devices: a whole 4x8x8 slice. The times are simulated.
512 devices in a mesh: row: 32 (over z, x), col: 16 (over y, core).
Axes of the slice: x: 4, y: 8, z: 8, core: 2. Of those that a mesh axis runs over, the one named last changes fastest.
Arguments:
- coeffs: float32 [4096, 128], P(('row', 'col')), may hold values from -6 to 6
- basis: float32 [256, 128, 4096], P('row', 'col'), may hold values from -0.1875 to 0.1875
- observed: float32 [256, 128, 128], P('row', 'col'), may hold values from -6 to 6
- lift_w: float32 [32], replicated, may hold values from -3 to 3
- lift_b: float32 [32], replicated, may hold values from -3 to 3
- w_one: bfloat16 [3, 3, 32, 32], replicated, may hold values from -0.375 to 0.375
- b_one: float32 [32], replicated, may hold values from -3 to 3
- w_two: bfloat16 [3, 3, 32, 32], replicated, may hold values from -0.375 to 0.375
- b_two: float32 [32], replicated, may hold values from -3 to 3
- read_w: float32 [32], replicated, may hold values from -1 to 1
Outputs:
- pressure: float32 [256, 128, 128], P('row', 'col')
- grad_coeffs: float32 [4096, 128], P(('row', 'col'))
All inputs are finite; a program needn't handle non-finite values.
Results may differ from a plain program's by a relative error of at most 0.015.
Values may be sent and summed in bfloat16 or wider, within the bound.
No kernel may reach another device: no remote copies, remote signals or barrier semaphores. Data moves between devices by JAX's collectives and lax.ppermute only.
A program may use at most 64 MiB of HBM per device.

v0:
```python
import jax
import jax.numpy as jnp
from jax import lax
from jax.sharding import PartitionSpec as P

prior_weight = 0.1


def with_halo(block, sides, width):
    for axis, dim in sides:
        count = lax.axis_size(axis)
        forward = [(i, i + 1) for i in range(count - 1)]
        backward = [(target, source) for source, target in forward]
        low = lax.ppermute(
            lax.slice_in_dim(block, block.shape[dim] - width, None, axis=dim), axis, forward
        )
        high = lax.ppermute(lax.slice_in_dim(block, 0, width, axis=dim), axis, backward)
        block = jnp.concatenate([low, block, high], axis=dim)
    return block


def extend_tile(values):
    return with_halo(values, (("row", 0), ("col", 1)), 1)


def conv_fwd(values, weights, extend):
    padded = extend(values)
    nrow = values.shape[0]
    ncol = values.shape[1]
    running = jnp.zeros(values.shape[:3] + (weights.shape[3],), jnp.float32)
    for shift_x in range(3):
        for shift_y in range(3):
            window = padded[shift_x : shift_x + nrow, shift_y : shift_y + ncol]
            running = running + jnp.einsum(
                "xybi,io->xybo",
                window,
                weights[shift_x, shift_y],
                preferred_element_type=jnp.float32,
            )
    return running


def conv_back(grads, weights, extend):
    padded = extend(grads)
    nrow = grads.shape[0]
    ncol = grads.shape[1]
    running = jnp.zeros(grads.shape[:3] + (weights.shape[2],), jnp.float32)
    for shift_x in range(3):
        for shift_y in range(3):
            window = padded[2 - shift_x : 2 - shift_x + nrow, 2 - shift_y : 2 - shift_y + ncol]
            running = running + jnp.einsum(
                "xybo,io->xybi",
                window,
                weights[shift_x, shift_y],
                preferred_element_type=jnp.float32,
            )
    return running


def surrogate(logperm, observed, lift_w, lift_b, w_one, b_one, w_two, b_two, read_w, extend):
    lifted = (logperm[..., None] * lift_w + lift_b).astype(jnp.bfloat16)
    hidden_one = jnp.tanh(conv_fwd(lifted, w_one, extend) + b_one).astype(jnp.bfloat16)
    hidden_two = jnp.tanh(conv_fwd(hidden_one, w_two, extend) + b_two)
    pressure = jnp.sum(hidden_two * read_w, axis=-1)
    misfit = pressure - observed
    grad_two = (misfit[..., None] * read_w * (1.0 - hidden_two * hidden_two)).astype(jnp.bfloat16)
    h_one = hidden_one.astype(jnp.float32)
    grad_one = (conv_back(grad_two, w_two, extend) * (1.0 - h_one * h_one)).astype(jnp.bfloat16)
    grad_field = jnp.sum(conv_back(grad_one, w_one, extend) * lift_w, axis=-1)
    return (pressure, grad_field)


def shards(coeffs, basis, observed, lift_w, lift_b, w_one, b_one, w_two, b_two, read_w):
    tile_rows, tile_cols, mode_count = basis.shape
    batch_size = coeffs.shape[1]
    flat_basis = basis.reshape(tile_rows * tile_cols, mode_count)
    basis_part = flat_basis
    logperm = jnp.dot(
        basis_part,
        lax.all_gather(coeffs, ("row", "col"), axis=0, tiled=True),
        precision=lax.Precision.HIGHEST,
        preferred_element_type=jnp.float32,
    )
    logperm = logperm.reshape(tile_rows, tile_cols, batch_size)
    pressure, grad_field = surrogate(
        logperm, observed, lift_w, lift_b, w_one, b_one, w_two, b_two, read_w, extend_tile
    )
    grad_flat = grad_field.reshape(tile_rows * tile_cols, batch_size)
    basis_part = flat_basis
    summed = lax.psum_scatter(
        lax.dot_general(
            basis_part,
            grad_flat,
            (((0,), (0,)), ((), ())),
            precision=lax.Precision.HIGHEST,
            preferred_element_type=jnp.float32,
        ),
        ("row", "col"),
        scatter_dimension=0,
        tiled=True,
    )
    grad_coeffs = summed + prior_weight * coeffs
    return (pressure, grad_coeffs)


def solution(mesh):
    return jax.shard_map(
        shards,
        mesh=mesh,
        in_specs=(
            P(("row", "col"), None),
            P("row", "col", None),
            P("row", "col", None),
            P(),
            P(),
            P(),
            P(),
            P(),
            P(),
            P(),
        ),
        out_specs=(P("row", "col", None), P(("row", "col"), None)),
        check_vma=False,
    )
```

profile of v0, /device:TPU:1, one launch (start us, length us, event | category | flops | bytes accessed | tf_op | source)
XLA Modules:
  0.0 521.0 jit_solution(12413397913941933140)
XLA Ops:
  7.2 0.7 all-gather.2.cloned.1.call-update
  8.0 126.0 %all-gather.2.cloned.1.call-done = f32[4096,128]{1,0:T(8,128)} async-done(((f32[8,128]{1,0:T(8,128)}), f32[4096,128]{1,0:T(8,128)}) %all-gather.2.cloned.1.call-update) | async-done | bytes 2097168 | tf_op jit(solution)/shard_map/all_gather | solution.py:80
  134.0 3.0 fusion
  137.2 3.0 collective-permute-start
  140.3 1.3 collective-permute-start.1
  141.6 0.4 fusion.115
  142.0 3.3 collective-permute-done.1
  145.3 4.7 collective-permute-start.2
  150.0 1.9 collective-permute-start.3
  151.9 0.3 fusion.76
  152.2 0.3 fusion.67
  152.6 3.2 collective-permute-done.3
  155.9 0.3 fusion.74
  156.2 0.3 fusion.65
  156.5 0.3 fusion.72
  156.8 0.3 fusion.69
  157.2 0.4 fusion.21
  157.8 0.5 fusion.32
  158.3 3.1 collective-permute-start.4
  161.4 1.3 collective-permute-start.5
  162.7 0.3 fusion.91
  163.1 3.4 collective-permute-done.5
  166.5 3.9 collective-permute-start.6
  170.4 1.9 collective-permute-start.7
  172.3 0.3 fusion.62
  172.6 0.3 fusion.53
  172.9 3.2 collective-permute-done.7
  176.3 0.3 fusion.60
  176.6 0.3 fusion.51
  176.9 0.3 fusion.58
  177.2 0.3 fusion.55
  177.6 0.5 fusion.27
  178.2 0.5 multiply_reduce_fusion
  179.3 1.3 collective-permute-start.9
  180.6 4.0 collective-permute-start.8
  184.6 0.3 fusion.89
  184.9 1.0 collective-permute-done.8
  185.9 3.0 collective-permute-start.11
  188.9 1.9 collective-permute-start.10
  190.8 0.3 fusion.35
  191.1 0.3 fusion.39
  191.4 3.3 collective-permute-done.10
  194.6 0.3 fusion.93
  194.9 0.3 fusion.84
  195.5 0.3 fusion.79
  195.8 0.3 fusion.15
  196.1 0.5 fusion.33
  196.6 1.3 collective-permute-start.13
  197.9 4.7 collective-permute-start.12
  202.6 0.3 fusion.113
  202.9 1.0 collective-permute-done.12
  204.0 2.7 collective-permute-start.15
  206.6 2.1 collective-permute-start.14
  208.7 0.3 fusion.43
  209.0 0.3 fusion.47
  209.3 3.1 collective-permute-done.14
  212.7 0.3 fusion.108
  212.9 0.3 fusion.120
  213.5 0.3 fusion.8
  213.8 0.5 fusion.34
  214.3 3.2 convolution_bitcast_fusion
  217.5 295.0 %all-reduce.3.cloned.1.call-done = f32[4096,128]{0,1:T(8,128)} async-done(((f32[4096,128]{0,1:T(8,128)}), f32[4096,128]{0,1:T(8,128)}) %all-reduce.3.cloned.1.call-update) | async-done | bytes 2097168
  512.5 0.9 constant_dynamic-slice_fusion
  513.5 0.6 multiply_add_fusion
  (50 shorter events, 2.5 us)
Async XLA Ops:
  7.2 126.9 %copy-start = (f32[8,8,4096]{2,1,0:T(8,128)S(1)}, f32[8,8,4096]{2,1,0:T(8,128)}, u32[]{:S(2)}) copy-start(f32[8,8,4096]{2,1,0:T(8,128)} %param.11) | copy-start | bytes 3145732
  7.2 126.8 %all-gather.2.cloned.1.call-start = ((), (), s32[]{:S(2)}) async-start(), calls=%async_computation | async-start | bytes 2101248 | tf_op jit(solution)/shard_map/all_gather | solution.py:80
  7.9 129.1 %copy-start.6 = (f32[32]{0:T(128)S(1)}, f32[32]{0:T(128)}, u32[]{:S(2)}) copy-start(f32[32]{0:T(128)} %param.13) | copy-start | bytes 388
  7.9 129.1 %copy-start.7 = (f32[32]{0:T(128)S(1)}, f32[32]{0:T(128)}, u32[]{:S(2)}) copy-start(f32[32]{0:T(128)} %param.14) | copy-start | bytes 388
  7.9 133.6 %copy-start.2 = (bf16[3,3,32,32]{3,2,1,0:T(8,128)(2,1)S(1)}, bf16[3,3,32,32]{3,2,1,0:T(8,128)(2,1)}, u32[]{:S(2)}) copy-start(bf16[3,3,32,32]{3,2,1,0:T(8,128)(2,1)} %param.15) | copy-start | bytes 55300
  7.9 504.6 %all-reduce.3.cloned.1.call-start = ((), (), s32[]{:S(2)}) async-start(), calls=%async_computation.1 | async-start | bytes 4194304
  137.2 4.7 collective-permute-start
  140.3 5.0 collective-permute-start.1
  145.3 7.2 %collective-permute-start.2 = (bf16[10,1,128,32]{2,3,1,0:T(8,128)(2,1)S(1)}, bf16[10,1,128,32]{2,3,1,0:T(8,128)(2,1)S(1)}, u32[]{:S(2)}, u32[]{:S(2)}) collective-permute-start(bf16[10,1,128,32]{2,3,1,0:T(8,128)(2,1)S(1)} %get-tuple-element.16), channel_id=1, source_target_pairs={{0,1},{1,2},{2,3},{3,4},{4,5},{5,6},{6,7},{7,8},{8,9},{9,10},{10,1... | collective-permute-start | bytes 245768 | tf_op jit(solution)/shard_map/ppermute | solution.py:14
  150.0 5.8 %collective-permute-start.3 = (bf16[10,1,128,32]{2,3,1,0:T(8,128)(2,1)S(1)}, bf16[10,1,128,32]{2,3,1,0:T(8,128)(2,1)S(1)}, u32[]{:S(2)}, u32[]{:S(2)}) collective-permute-start(bf16[10,1,128,32]{2,3,1,0:T(8,128)(2,1)S(1)} %get-tuple-element.17), channel_id=1, source_target_pairs={{1,0},{2,1},{3,2},{4,3},{5,4},{6,5},{7,6},{8,7},{9,8},{10,9},{11,1... | collective-permute-start | bytes 245768 | tf_op jit(solution)/shard_map/ppermute | solution.py:17
  157.2 0.7 copy-start.10
  157.8 4.9 copy-start.1
  158.3 4.7 collective-permute-start.4
  161.4 5.0 collective-permute-start.5
  166.5 6.5 %collective-permute-start.6 = (bf16[10,1,128,32]{2,3,1,0:T(8,128)(2,1)S(1)}, bf16[10,1,128,32]{2,3,1,0:T(8,128)(2,1)S(1)}, u32[]{:S(2)}, u32[]{:S(2)}) collective-permute-start(bf16[10,1,128,32]{2,3,1,0:T(8,128)(2,1)S(1)} %get-tuple-element.12), channel_id=1, source_target_pairs={{0,1},{1,2},{2,3},{3,4},{4,5},{5,6},{6,7},{7,8},{8,9},{9,10},{10,1... | collective-permute-start | bytes 245768 | tf_op jit(solution)/shard_map/ppermute | solution.py:14
  170.4 5.8 %collective-permute-start.7 = (bf16[10,1,128,32]{2,3,1,0:T(8,128)(2,1)S(1)}, bf16[10,1,128,32]{2,3,1,0:T(8,128)(2,1)S(1)}, u32[]{:S(2)}, u32[]{:S(2)}) collective-permute-start(bf16[10,1,128,32]{2,3,1,0:T(8,128)(2,1)S(1)} %get-tuple-element.13), channel_id=1, source_target_pairs={{1,0},{2,1},{3,2},{4,3},{5,4},{6,5},{7,6},{8,7},{9,8},{10,9},{11,1... | collective-permute-start | bytes 245768 | tf_op jit(solution)/shard_map/ppermute | solution.py:17
  177.6 0.7 copy-start.8
  177.6 0.7 copy-start.9
  178.2 0.8 copy-start.4
  178.8 6.1 %copy-start.3 = (f32[8,8,128]{2,1,0:T(8,128)}, f32[8,8,128]{2,1,0:T(8,128)S(1)}, u32[]{:S(2)}) copy-start(f32[8,8,128]{2,1,0:T(8,128)S(1)} %get-tuple-element.26) | copy-start | bytes 98308
  179.3 5.6 %collective-permute-start.9 = (bf16[1,8,128,32]{2,3,1,0:T(8,128)(2,1)S(1)}, bf16[1,8,128,32]{2,3,1,0:T(8,128)(2,1)S(1)}, u32[]{:S(2)}, u32[]{:S(2)}) collective-permute-start(bf16[1,8,128,32]{2,3,1,0:T(8,128)(2,1)S(1)} %get-tuple-element.21), channel_id=1, source_target_pairs={{16,0},{32,16},{48,32},{64,48},{80,64},{96,80},{112,96},{128,112},... | collective-permute-start | bytes 196616 | tf_op jit(solution)/shard_map/ppermute | solution.py:17
  180.6 5.3 %collective-permute-start.8 = (bf16[1,8,128,32]{2,3,1,0:T(8,128)(2,1)S(1)}, bf16[1,8,128,32]{2,3,1,0:T(8,128)(2,1)S(1)}, u32[]{:S(2)}, u32[]{:S(2)}) collective-permute-start(bf16[1,8,128,32]{2,3,1,0:T(8,128)(2,1)S(1)} %get-tuple-element.20), channel_id=1, source_target_pairs={{0,16},{16,32},{32,48},{48,64},{64,80},{80,96},{96,112},{112,128},... | collective-permute-start | bytes 196616 | tf_op jit(solution)/shard_map/ppermute | solution.py:14
  185.9 9.3 %collective-permute-start.11 = (bf16[10,1,128,32]{2,3,1,0:T(8,128)(2,1)S(1)}, bf16[10,1,128,32]{2,3,1,0:T(8,128)(2,1)S(1)}, u32[]{:S(2)}, u32[]{:S(2)}) collective-permute-start(bf16[10,1,128,32]{2,3,1,0:T(8,128)(2,1)S(1)} %get-tuple-element.9), channel_id=1, source_target_pairs={{0,1},{1,2},{2,3},{3,4},{4,5},{5,6},{6,7},{7,8},{8,9},{9,10},{10,1... | collective-permute-start | bytes 245768 | tf_op jit(solution)/shard_map/ppermute | solution.py:14
  188.9 5.8 %collective-permute-start.10 = (bf16[10,1,128,32]{2,3,1,0:T(8,128)(2,1)S(1)}, bf16[10,1,128,32]{2,3,1,0:T(8,128)(2,1)S(1)}, u32[]{:S(2)}, u32[]{:S(2)}) collective-permute-start(bf16[10,1,128,32]{2,3,1,0:T(8,128)(2,1)S(1)} %get-tuple-element.8), channel_id=1, source_target_pairs={{1,0},{2,1},{3,2},{4,3},{5,4},{6,5},{7,6},{8,7},{9,8},{10,9},{11,1... | collective-permute-start | bytes 245768 | tf_op jit(solution)/shard_map/ppermute | solution.py:17
  196.6 6.3 %collective-permute-start.13 = (bf16[1,8,128,32]{2,3,1,0:T(8,128)(2,1)S(1)}, bf16[1,8,128,32]{2,3,1,0:T(8,128)(2,1)S(1)}, u32[]{:S(2)}, u32[]{:S(2)}) collective-permute-start(bf16[1,8,128,32]{2,3,1,0:T(8,128)(2,1)S(1)} %get-tuple-element.19), channel_id=1, source_target_pairs={{16,0},{32,16},{48,32},{64,48},{80,64},{96,80},{112,96},{128,112},... | collective-permute-start | bytes 196616 | tf_op jit(solution)/shard_map/ppermute | solution.py:17
  197.9 6.0 %collective-permute-start.12 = (bf16[1,8,128,32]{2,3,1,0:T(8,128)(2,1)S(1)}, bf16[1,8,128,32]{2,3,1,0:T(8,128)(2,1)S(1)}, u32[]{:S(2)}, u32[]{:S(2)}) collective-permute-start(bf16[1,8,128,32]{2,3,1,0:T(8,128)(2,1)S(1)} %get-tuple-element.18), channel_id=1, source_target_pairs={{0,16},{16,32},{32,48},{48,64},{64,80},{80,96},{96,112},{112,128},... | collective-permute-start | bytes 196616 | tf_op jit(solution)/shard_map/ppermute | solution.py:14
  204.0 9.0 %collective-permute-start.15 = (bf16[10,1,128,32]{2,3,1,0:T(8,128)(2,1)S(1)}, bf16[10,1,128,32]{2,3,1,0:T(8,128)(2,1)S(1)}, u32[]{:S(2)}, u32[]{:S(2)}) collective-permute-start(bf16[10,1,128,32]{2,3,1,0:T(8,128)(2,1)S(1)} %get-tuple-element.7), channel_id=1, source_target_pairs={{0,1},{1,2},{2,3},{3,4},{4,5},{5,6},{6,7},{7,8},{8,9},{9,10},{10,1... | collective-permute-start | bytes 245768 | tf_op jit(solution)/shard_map/ppermute | solution.py:14
  206.6 5.8 %collective-permute-start.14 = (bf16[10,1,128,32]{2,3,1,0:T(8,128)(2,1)S(1)}, bf16[10,1,128,32]{2,3,1,0:T(8,128)(2,1)S(1)}, u32[]{:S(2)}, u32[]{:S(2)}) collective-permute-start(bf16[10,1,128,32]{2,3,1,0:T(8,128)(2,1)S(1)} %get-tuple-element.6), channel_id=1, source_target_pairs={{1,0},{2,1},{3,2},{4,3},{5,4},{6,5},{7,6},{8,7},{9,8},{10,9},{11,1... | collective-permute-start | bytes 245768 | tf_op jit(solution)/shard_map/ppermute | solution.py:17
  217.5 296.0 %copy-start.5 = (f32[8,128]{1,0:T(8,128)S(1)}, f32[8,128]{1,0:T(8,128)}, u32[]{:S(2)}) copy-start(f32[8,128]{1,0:T(8,128)} %param.10) | copy-start | bytes 12292
Sparse Core Ops, SparseCore 0:
  12.2 121.8 all-gather.1
  217.6 294.8 all-reduce.2
where the time goes:
time: 522 us; the launch traced here: 521 us
  waiting for transfers between devices  443 us (85%)
  starting transfers between devices  42.1 us (8%)
  matrix products  18 us (3%)
  between operations  14.6 us (3%)
    unnamed x3, waiting for transfers between devices  296 us
    all_gather x1, waiting for transfers between devices, shards(): lax.all_gather(coeffs, ('row', 'col'), axis=0, tiled=True)  126 us
    ppermute x8, starting transfers between devices, with_halo(): lax.ppermute(lax.slice_in_dim(block, block.shape[dim] - width, None, axis...  29 us
    ppermute x8, waiting for transfers between devices, with_halo(): lax.ppermute(lax.slice_in_dim(block, 0, width, axis=dim), axis, backward)  19.4 us
    ppermute x8, starting transfers between devices, with_halo(): lax.ppermute(lax.slice_in_dim(block, 0, width, axis=dim), axis, backward)  13 us
  transfers between devices with their start and end apart: 18, of which 10 were waited for; matrix products, arithmetic and copies ran while one was open for 1% of the time, Pallas kernels for 0%

commit v1 on v0

--- a/solution.py
+++ b/solution.py
@@ -75,9 +75,22 @@
     batch_size = coeffs.shape[1]
     flat_basis = basis.reshape(tile_rows * tile_cols, mode_count)
     basis_part = flat_basis
+
+    def _balance_task(obj):
+        main = jnp.concatenate(
+            lax.all_to_all(
+                jnp.stack([obj for _ in range(lax.axis_size(("row", "col")))], axis=0),
+                axis_name=("row", "col"),
+                split_axis=0,
+                concat_axis=0,
+            ),
+            axis=0,
+        )
+        return main
+
     logperm = jnp.dot(
         basis_part,
-        lax.all_gather(coeffs, ("row", "col"), axis=0, tiled=True),
+        _balance_task(coeffs),
         precision=lax.Precision.HIGHEST,
         preferred_element_type=jnp.float32,
     )

time: 522 us -> 469 us (0.90)
  waiting for transfers between devices: 443 us -> 316 us
  blocking collectives: 0 us -> 77 us
    all_gather x1 -> x0, waiting for transfers between devices: 126 us -> none  [shards(): lax.all_gather(coeffs, ('row', 'col'), axis=0, tiled=True)]
    all_to_all x0 -> x1, blocking collectives: none -> 77 us  [_balance_task(): lax.all_to_all(jnp.stack([obj for _ in range(lax.axis_size(('row', 'col')...]
    unnamed x3 -> x2, waiting for transfers between devices: 296 us -> 294 us
  transfers between devices with their start and end apart: 18 -> 17, of which waited for: 10 -> 9; matrix products, arithmetic and copies ran while one was open for 1% -> 1% of each run, Pallas kernels for 0% -> 0%
where the time goes in v1:
time: 469 us; the launch traced here: 468 us
  waiting for transfers between devices  316 us (67%)
  blocking collectives  77 us (16%)
  starting transfers between devices  40.6 us (9%)
  matrix products  16.3 us (3%)
  between operations  14.6 us (3%)
    unnamed x2, waiting for transfers between devices  294 us
    all_to_all x1, blocking collectives, _balance_task(): lax.all_to_all(jnp.stack([obj for _ in range(lax.axis_size(('row', 'col')...  77 us
    ppermute x8, starting transfers between devices, with_halo(): lax.ppermute(lax.slice_in_dim(block, block.shape[dim] - width, None, axis...  27.5 us
    ppermute x8, waiting for transfers between devices, with_halo(): lax.ppermute(lax.slice_in_dim(block, 0, width, axis=dim), axis, backward)  19.4 us
    ppermute x8, starting transfers between devices, with_halo(): lax.ppermute(lax.slice_in_dim(block, 0, width, axis=dim), axis, backward)  13 us
  transfers between devices with their start and end apart: 17, of which 9 were waited for; matrix products, arithmetic and copies ran while one was open for 1% of the time, Pallas kernels for 0%

profile of v1, /device:TPU:1, one launch (start us, length us, event | category | flops | bytes accessed | tf_op | source)
XLA Modules:
  0.0 468.3 jit_solution(9981590018778538026)
XLA Ops:
  7.2 0.9 stack.2
  8.1 77.0 %all_to_all.5 = f32[512,8,128]{2,1,0:T(8,128)S(1)} all-to-all(f32[512,8,128]{2,1,0:T(8,128)S(1)} %stack.2), channel_id=1, replica_groups=mesh['row'=32,'col'=16] {'row','col'}, dimensions={0} | all-to-all | bytes 4194304 | tf_op jit(solution)/shard_map/all_to_all | solution.py:81
  85.1 1.4 fusion
  86.8 2.6 collective-permute-start
  89.4 1.3 collective-permute-start.1
  90.7 0.4 fusion.115
  91.1 3.3 collective-permute-done.1
  94.4 4.4 collective-permute-start.2
  98.8 1.9 collective-permute-start.3
  100.7 0.3 fusion.76
  101.1 0.3 fusion.67
  101.4 3.2 collective-permute-done.3
  104.7 0.3 fusion.74
  105.0 0.3 fusion.65
  105.3 0.3 fusion.72
  105.7 0.3 fusion.69
  106.0 0.4 fusion.21
  106.6 0.5 fusion.32
  107.1 2.3 collective-permute-start.4
  109.5 1.3 collective-permute-start.5
  110.8 0.3 fusion.91
  111.1 3.4 collective-permute-done.5
  114.5 4.0 collective-permute-start.6
  118.5 1.9 collective-permute-start.7
  120.4 0.3 fusion.62
  120.7 0.3 fusion.53
  121.0 3.2 collective-permute-done.7
  124.4 0.3 fusion.60
  124.7 0.3 fusion.51
  125.0 0.3 fusion.58
  125.3 0.3 fusion.55
  125.7 0.4 fusion.27
  126.3 0.5 multiply_reduce_fusion
  127.4 1.3 collective-permute-start.9
  128.7 4.1 collective-permute-start.8
  132.7 0.3 fusion.89
  133.0 1.0 collective-permute-done.8
  134.1 2.9 collective-permute-start.11
  137.0 2.1 collective-permute-start.10
  139.1 0.3 fusion.35
  139.4 0.3 fusion.39
  139.7 3.1 collective-permute-done.10
  142.7 0.3 fusion.93
  143.0 0.3 fusion.84
  143.3 0.3 fusion.96
  143.9 0.3 fusion.15
  144.2 0.5 fusion.33
  144.7 1.3 collective-permute-start.13
  146.0 4.6 collective-permute-start.12
  150.7 0.3 fusion.113
  151.0 1.0 collective-permute-done.12
  152.0 2.7 collective-permute-start.15
  154.7 1.9 collective-permute-start.14
  156.6 0.3 fusion.43
  156.9 0.3 fusion.47
  157.2 3.3 collective-permute-done.14
  160.7 0.3 fusion.108
  161.0 0.3 fusion.120
  161.6 0.3 fusion.8
  161.9 0.5 fusion.34
  162.4 3.2 convolution_bitcast_fusion
  165.6 294.3 %all-reduce.3.cloned.1.call-done = f32[4096,128]{0,1:T(8,128)} async-done(((f32[4096,128]{0,1:T(8,128)}), f32[4096,128]{0,1:T(8,128)}) %all-reduce.3.cloned.1.call-update) | async-done | bytes 2097168
  459.9 0.9 constant_dynamic-slice_fusion
  460.9 0.6 multiply_add_fusion
  (49 shorter events, 2.5 us)
Async XLA Ops:
  7.2 78.0 %copy-start = (f32[8,8,4096]{2,1,0:T(8,128)S(1)}, f32[8,8,4096]{2,1,0:T(8,128)}, u32[]{:S(2)}) copy-start(f32[8,8,4096]{2,1,0:T(8,128)} %param.11) | copy-start | bytes 3145732
  7.2 452.7 %all-reduce.3.cloned.1.call-start = ((), (), s32[]{:S(2)}) async-start(), calls=%async_computation.1 | async-start | bytes 4194304
  85.1 1.4 copy-start.6
  85.1 1.4 copy-start.7
  85.1 5.5 %copy-start.2 = (bf16[3,3,32,32]{3,2,1,0:T(8,128)(2,1)S(1)}, bf16[3,3,32,32]{3,2,1,0:T(8,128)(2,1)}, u32[]{:S(2)}) copy-start(bf16[3,3,32,32]{3,2,1,0:T(8,128)(2,1)} %param.15) | copy-start | bytes 55300
  86.8 4.3 collective-permute-start
  89.4 5.0 %collective-permute-start.1 = (bf16[1,8,128,32]{2,3,1,0:T(8,128)(2,1)S(1)}, bf16[1,8,128,32]{2,3,1,0:T(8,128)(2,1)S(1)}, u32[]{:S(2)}, u32[]{:S(2)}) collective-permute-start(bf16[1,8,128,32]{2,3,1,0:T(8,128)(2,1)S(1)} %get-tuple-element.25), channel_id=1, source_target_pairs={{16,0},{32,16},{48,32},{64,48},{80,64},{96,80},{112,96},{128,112},... | collective-permute-start | bytes 196616 | tf_op jit(solution)/shard_map/ppermute | solution.py:17
  94.4 7.0 %collective-permute-start.2 = (bf16[10,1,128,32]{2,3,1,0:T(8,128)(2,1)S(1)}, bf16[10,1,128,32]{2,3,1,0:T(8,128)(2,1)S(1)}, u32[]{:S(2)}, u32[]{:S(2)}) collective-permute-start(bf16[10,1,128,32]{2,3,1,0:T(8,128)(2,1)S(1)} %get-tuple-element.16), channel_id=1, source_target_pairs={{0,1},{1,2},{2,3},{3,4},{4,5},{5,6},{6,7},{7,8},{8,9},{9,10},{10,1... | collective-permute-start | bytes 245768 | tf_op jit(solution)/shard_map/ppermute | solution.py:14
  98.8 5.8 %collective-permute-start.3 = (bf16[10,1,128,32]{2,3,1,0:T(8,128)(2,1)S(1)}, bf16[10,1,128,32]{2,3,1,0:T(8,128)(2,1)S(1)}, u32[]{:S(2)}, u32[]{:S(2)}) collective-permute-start(bf16[10,1,128,32]{2,3,1,0:T(8,128)(2,1)S(1)} %get-tuple-element.17), channel_id=1, source_target_pairs={{1,0},{2,1},{3,2},{4,3},{5,4},{6,5},{7,6},{8,7},{9,8},{10,9},{11,1... | collective-permute-start | bytes 245768 | tf_op jit(solution)/shard_map/ppermute | solution.py:17
  106.0 0.7 copy-start.10
  106.6 4.1 copy-start.1
  107.1 4.0 collective-permute-start.4
  109.5 5.0 %collective-permute-start.5 = (bf16[1,8,128,32]{2,3,1,0:T(8,128)(2,1)S(1)}, bf16[1,8,128,32]{2,3,1,0:T(8,128)(2,1)S(1)}, u32[]{:S(2)}, u32[]{:S(2)}) collective-permute-start(bf16[1,8,128,32]{2,3,1,0:T(8,128)(2,1)S(1)} %get-tuple-element.23), channel_id=1, source_target_pairs={{16,0},{32,16},{48,32},{64,48},{80,64},{96,80},{112,96},{128,112},... | collective-permute-start | bytes 196616 | tf_op jit(solution)/shard_map/ppermute | solution.py:17
  114.5 6.5 %collective-permute-start.6 = (bf16[10,1,128,32]{2,3,1,0:T(8,128)(2,1)S(1)}, bf16[10,1,128,32]{2,3,1,0:T(8,128)(2,1)S(1)}, u32[]{:S(2)}, u32[]{:S(2)}) collective-permute-start(bf16[10,1,128,32]{2,3,1,0:T(8,128)(2,1)S(1)} %get-tuple-element.12), channel_id=1, source_target_pairs={{0,1},{1,2},{2,3},{3,4},{4,5},{5,6},{6,7},{7,8},{8,9},{9,10},{10,1... | collective-permute-start | bytes 245768 | tf_op jit(solution)/shard_map/ppermute | solution.py:14
  118.5 5.8 %collective-permute-start.7 = (bf16[10,1,128,32]{2,3,1,0:T(8,128)(2,1)S(1)}, bf16[10,1,128,32]{2,3,1,0:T(8,128)(2,1)S(1)}, u32[]{:S(2)}, u32[]{:S(2)}) collective-permute-start(bf16[10,1,128,32]{2,3,1,0:T(8,128)(2,1)S(1)} %get-tuple-element.13), channel_id=1, source_target_pairs={{1,0},{2,1},{3,2},{4,3},{5,4},{6,5},{7,6},{8,7},{9,8},{10,9},{11,1... | collective-permute-start | bytes 245768 | tf_op jit(solution)/shard_map/ppermute | solution.py:17
  125.6 0.7 copy-start.8
  125.7 0.7 copy-start.9
  126.3 0.8 copy-start.4
  126.9 6.1 %copy-start.3 = (f32[8,8,128]{2,1,0:T(8,128)}, f32[8,8,128]{2,1,0:T(8,128)S(1)}, u32[]{:S(2)}) copy-start(f32[8,8,128]{2,1,0:T(8,128)S(1)} %get-tuple-element.26) | copy-start | bytes 98308
  127.4 5.7 %collective-permute-start.9 = (bf16[1,8,128,32]{2,3,1,0:T(8,128)(2,1)S(1)}, bf16[1,8,128,32]{2,3,1,0:T(8,128)(2,1)S(1)}, u32[]{:S(2)}, u32[]{:S(2)}) collective-permute-start(bf16[1,8,128,32]{2,3,1,0:T(8,128)(2,1)S(1)} %get-tuple-element.21), channel_id=1, source_target_pairs={{16,0},{32,16},{48,32},{64,48},{80,64},{96,80},{112,96},{128,112},... | collective-permute-start | bytes 196616 | tf_op jit(solution)/shard_map/ppermute | solution.py:17
  128.7 5.4 %collective-permute-start.8 = (bf16[1,8,128,32]{2,3,1,0:T(8,128)(2,1)S(1)}, bf16[1,8,128,32]{2,3,1,0:T(8,128)(2,1)S(1)}, u32[]{:S(2)}, u32[]{:S(2)}) collective-permute-start(bf16[1,8,128,32]{2,3,1,0:T(8,128)(2,1)S(1)} %get-tuple-element.20), channel_id=1, source_target_pairs={{0,16},{16,32},{32,48},{48,64},{64,80},{80,96},{96,112},{112,128},... | collective-permute-start | bytes 196616 | tf_op jit(solution)/shard_map/ppermute | solution.py:14
  134.1 9.3 %collective-permute-start.11 = (bf16[10,1,128,32]{2,3,1,0:T(8,128)(2,1)S(1)}, bf16[10,1,128,32]{2,3,1,0:T(8,128)(2,1)S(1)}, u32[]{:S(2)}, u32[]{:S(2)}) collective-permute-start(bf16[10,1,128,32]{2,3,1,0:T(8,128)(2,1)S(1)} %get-tuple-element.9), channel_id=1, source_target_pairs={{0,1},{1,2},{2,3},{3,4},{4,5},{5,6},{6,7},{7,8},{8,9},{9,10},{10,1... | collective-permute-start | bytes 245768 | tf_op jit(solution)/shard_map/ppermute | solution.py:14
  137.0 5.8 %collective-permute-start.10 = (bf16[10,1,128,32]{2,3,1,0:T(8,128)(2,1)S(1)}, bf16[10,1,128,32]{2,3,1,0:T(8,128)(2,1)S(1)}, u32[]{:S(2)}, u32[]{:S(2)}) collective-permute-start(bf16[10,1,128,32]{2,3,1,0:T(8,128)(2,1)S(1)} %get-tuple-element.8), channel_id=1, source_target_pairs={{1,0},{2,1},{3,2},{4,3},{5,4},{6,5},{7,6},{8,7},{9,8},{10,9},{11,1... | collective-permute-start | bytes 245768 | tf_op jit(solution)/shard_map/ppermute | solution.py:17
  144.7 6.2 %collective-permute-start.13 = (bf16[1,8,128,32]{2,3,1,0:T(8,128)(2,1)S(1)}, bf16[1,8,128,32]{2,3,1,0:T(8,128)(2,1)S(1)}, u32[]{:S(2)}, u32[]{:S(2)}) collective-permute-start(bf16[1,8,128,32]{2,3,1,0:T(8,128)(2,1)S(1)} %get-tuple-element.19), channel_id=1, source_target_pairs={{16,0},{32,16},{48,32},{64,48},{80,64},{96,80},{112,96},{128,112},... | collective-permute-start | bytes 196616 | tf_op jit(solution)/shard_map/ppermute | solution.py:17
  146.0 6.0 %collective-permute-start.12 = (bf16[1,8,128,32]{2,3,1,0:T(8,128)(2,1)S(1)}, bf16[1,8,128,32]{2,3,1,0:T(8,128)(2,1)S(1)}, u32[]{:S(2)}, u32[]{:S(2)}) collective-permute-start(bf16[1,8,128,32]{2,3,1,0:T(8,128)(2,1)S(1)} %get-tuple-element.18), channel_id=1, source_target_pairs={{0,16},{16,32},{32,48},{48,64},{64,80},{80,96},{96,112},{112,128},... | collective-permute-start | bytes 196616 | tf_op jit(solution)/shard_map/ppermute | solution.py:14
  152.0 9.0 %collective-permute-start.15 = (bf16[10,1,128,32]{2,3,1,0:T(8,128)(2,1)S(1)}, bf16[10,1,128,32]{2,3,1,0:T(8,128)(2,1)S(1)}, u32[]{:S(2)}, u32[]{:S(2)}) collective-permute-start(bf16[10,1,128,32]{2,3,1,0:T(8,128)(2,1)S(1)} %get-tuple-element.7), channel_id=1, source_target_pairs={{0,1},{1,2},{2,3},{3,4},{4,5},{5,6},{6,7},{7,8},{8,9},{9,10},{10,1... | collective-permute-start | bytes 245768 | tf_op jit(solution)/shard_map/ppermute | solution.py:14
  154.7 5.8 %collective-permute-start.14 = (bf16[10,1,128,32]{2,3,1,0:T(8,128)(2,1)S(1)}, bf16[10,1,128,32]{2,3,1,0:T(8,128)(2,1)S(1)}, u32[]{:S(2)}, u32[]{:S(2)}) collective-permute-start(bf16[10,1,128,32]{2,3,1,0:T(8,128)(2,1)S(1)} %get-tuple-element.6), channel_id=1, source_target_pairs={{1,0},{2,1},{3,2},{4,3},{5,4},{6,5},{7,6},{8,7},{9,8},{10,9},{11,1... | collective-permute-start | bytes 245768 | tf_op jit(solution)/shard_map/ppermute | solution.py:17
  165.5 295.3 %copy-start.5 = (f32[8,128]{1,0:T(8,128)S(1)}, f32[8,128]{1,0:T(8,128)}, u32[]{:S(2)}) copy-start(f32[8,128]{1,0:T(8,128)} %param.10) | copy-start | bytes 12292
Sparse Core Ops, SparseCore 0:
  165.7 294.1 all-reduce.2
